TPU v7x, 256 devices: a whole 4x4x8 slice. The times are simulated.
256 devices in a mesh: runs: 32 (over y, x, core), cells: 8 (over z).
Axes of the slice: x: 4, y: 4, z: 8, core: 2. Of those that a mesh axis runs over, the one named last changes fastest.
Arguments:
- train_depth: bfloat16 [16384, 32768], P('runs', 'cells'), may hold values from -6 to 6
- train_basis: bfloat16 [16384, 512], P('runs', 'cells'), may hold values from -6 to 6
- sample_basis: bfloat16 [16384, 512], P('runs', 'cells'), may hold values from -0.25 to 0.25
- gram_inverse: float32 [512, 512], replicated, may hold values from -8 to 8
Outputs:
- peak_depth: bfloat16 [16384, 32768], P('runs', 'cells')
All inputs are finite; a program needn't handle non-finite values.
Results may differ from a plain program's by a relative error of at most 0.0049.
Values may be sent and summed in bfloat16 or wider, within the bound.
No kernel may reach another device: no remote copies, remote signals or barrier semaphores. Data moves between devices by JAX's collectives and lax.ppermute only.
A program may use at most 64 MiB of HBM per device.

v0:
```python
import math
import jax
import jax.numpy as jnp
from jax import lax
from jax.sharding import PartitionSpec as P


def per_device(train_depth, train_basis, sample_basis, gram_inverse):
    terms_here = train_basis.shape[1]
    n_cells = lax.axis_size("cells")
    total_runs = train_depth.shape[0] * lax.axis_size("runs")
    norm_scale = 1.0 / math.sqrt(total_runs)
    both = jnp.concatenate([train_basis, sample_basis], axis=1).T
    both_full = lax.all_gather(both, "cells", axis=0, tiled=False)
    train_t = both_full[:, :terms_here, :].reshape(n_cells * terms_here, -1)
    sample_t = both_full[:, terms_here:, :].reshape(n_cells * terms_here, -1)
    partial_t = lax.dot_general(
        train_depth, train_t, (((0,), (1,)), ((), ())), preferred_element_type=jnp.float32
    )
    moments_t = lax.psum_scatter(partial_t, "runs", scatter_dimension=0, tiled=True) * norm_scale
    coeffs_t = lax.dot_general(
        moments_t, gram_inverse, (((1,), (1,)), ((), ())), precision=lax.Precision.HIGHEST
    ).astype(jnp.bfloat16)
    coeffs_full_t = lax.all_gather(coeffs_t, "runs", axis=0, tiled=True)
    peak_depth = lax.dot_general(
        sample_t, coeffs_full_t, (((0,), (1,)), ((), ())), preferred_element_type=jnp.float32
    ).astype(jnp.bfloat16)
    return peak_depth


def solution(mesh):
    in_specs = (P("runs", "cells"), P("runs", "cells"), P("runs", "cells"), P())
    out_specs = P("runs", "cells")
    return jax.shard_map(
        per_device, mesh=mesh, in_specs=in_specs, out_specs=out_specs, check_vma=False
    )
```

profile of v0, /device:TPU:1, one launch (start us, length us, event | category | flops | bytes accessed | tf_op | source)
XLA Modules:
  0.0 226.3 jit_solution(17582883952233589478)
XLA Ops:
  6.5 0.0 copy-start
  6.5 0.0 all-gather.6.cloned.1.call-start
  6.5 1.6 maximum_bitcast_fusion
  8.2 0.0 all-gather.6.cloned.1.call-update
  8.2 0.0 reduce-scatter.2.cloned.1.call-start
  8.2 38.1 %all-gather.6.cloned.1.call-done = bf16[1024,512]{1,0:T(8,128)(2,1)} async-done(((bf16[128,512]{1,0:T(8,128)(2,1)}), bf16[1024,512]{1,0:T(8,128)(2,1)}) %all-gather.6.cloned.1.call-update) | async-done | bytes 1048592 | tf_op jit(solution)/shard_map/all_gather | solution.py:14
  46.3 1.3 fusion.3
  47.6 7.8 %convolution_bitcast_fusion = f32[4096,512]{0,1:T(8,128)} fusion(bf16[512,512]{1,0:T(8,128)(2,1)S(1)} %bitcast.12, bf16[512,4096]{1,0:T(8,128)(2,1)} %param.4), kind=kOutput, calls=%fused_computation | convolution fusion | flops 2147483648 | bytes 13107200 | tf_op jit(solution)/shard_map/dot_general | solution.py:17
  55.4 0.0 reduce-scatter.2.cloned.1.call-update
  55.5 0.0 all-gather.4.cloned.1.call-start
  55.5 102.1 %reduce-scatter.2.cloned.1.call-done = f32[128,512]{0,1:T(8,128)} async-done(((f32[4096,512]{0,1:T(8,128)}), f32[128,512]{0,1:T(8,128)}) %reduce-scatter.2.cloned.1.call-update) | async-done | bytes 262160 | tf_op jit(solution)/shard_map/reduce_scatter | solution.py:20
  157.6 0.0 copy-done
  157.7 2.9 %convolution_convert_fusion.1 = bf16[128,512]{1,0:T(8,128)(2,1)} fusion(f32[512,512]{1,0:T(8,128)S(1)} %copy-done, f32[128,512]{0,1:T(8,128)} %reduce-scatter.2.cloned.1.call-done), kind=kOutput, calls=%fused_computation.2 | convolution fusion | flops 402784256 | bytes 1441792 | tf_op jit(solution)/shard_map/dot_general | solution.py:21
  160.5 0.0 all-gather.4.cloned.1.call-update
  160.5 52.7 %all-gather.4.cloned.1.call-done = bf16[4096,512]{1,0:T(8,128)(2,1)} async-done(((bf16[128,512]{1,0:T(8,128)(2,1)}), bf16[4096,512]{1,0:T(8,128)(2,1)}) %all-gather.4.cloned.1.call-update) | async-done | bytes 4194320 | tf_op jit(solution)/shard_map/all_gather | solution.py:24
  213.2 6.6 %convolution_convert_fusion = bf16[512,4096]{1,0:T(8,128)(2,1)} fusion(bf16[512,512]{1,0:T(8,128)(2,1)S(1)} %bitcast.14, bf16[4096,512]{1,0:T(8,128)(2,1)} %all-gather.4.cloned.1.call-done), kind=kOutput, calls=%fused_computation.1 | convolution fusion | flops 2149580800 | bytes 8912896 | tf_op jit(solution)/shard_map/dot_general | solution.py:25
Async XLA Ops:
  6.5 151.1 %copy-start = (f32[512,512]{1,0:T(8,128)S(1)}, f32[512,512]{1,0:T(8,128)}, u32[]{:S(2)}) copy-start(f32[512,512]{1,0:T(8,128)} %param.7) | copy-start | bytes 3145732
  6.5 39.8 %all-gather.6.cloned.1.call-start = ((), (), s32[]{:S(2)}) async-start(), calls=%async_computation.3 | async-start | bytes 1179648 | tf_op jit(solution)/shard_map/all_gather | solution.py:14
  8.2 149.5 %reduce-scatter.2.cloned.1.call-start = ((), (), s32[]{:S(2)}) async-start(), calls=%async_computation.1 | async-start | bytes 8650752 | tf_op jit(solution)/shard_map/reduce_scatter | solution.py:20
  55.5 157.7 %all-gather.4.cloned.1.call-start = ((), (), s32[]{:S(2)}) async-start(), calls=%async_computation.2 | async-start | bytes 4325376 | tf_op jit(solution)/shard_map/all_gather | solution.py:24
Sparse Core Ops, SparseCore 0:
  9.1 37.1 all-gather.5
  55.6 102.0 reduce-scatter.1
  160.7 52.5 all-gather.3
where the time goes:
time: 227 us; the launch traced here: 226 us
  waiting for transfers between devices  193 us (85%)
  matrix products  17.3 us (8%)
  between operations  13.1 us (6%)
    reduce_scatter x1, waiting for transfers between devices, per_device(): lax.psum_scatter(partial_t, 'runs', scatter_dimension=0, tiled=True)  102 us
    all_gather x1, waiting for transfers between devices, per_device(): coeffs_full_t = lax.all_gather(coeffs_t, 'runs', axis=0, tiled=True)  52.7 us
    all_gather x1, waiting for transfers between devices, per_device(): both_full = lax.all_gather(both, 'cells', axis=0, tiled=False)  38.1 us
    dot_general x1, matrix products, per_device(): lax.dot_general(train_depth, train_t, (((0,), (1,)), ((), ())), preferred...  7.84 us
    dot_general x1, matrix products, per_device(): lax.dot_general(sample_t, coeffs_full_t, (((0,), (1,)), ((), ())), prefer...  6.6 us
  transfers between devices with their start and end apart: 3, of which 3 were waited for; matrix products, arithmetic and copies ran while one was open for 0% of the time, Pallas kernels for 0%

commit v1 on v0

--- a/solution.py
+++ b/solution.py
@@ -21,7 +21,9 @@
     coeffs_t = lax.dot_general(
         moments_t, gram_inverse, (((1,), (1,)), ((), ())), precision=lax.Precision.HIGHEST
     ).astype(jnp.bfloat16)
-    coeffs_full_t = lax.all_gather(coeffs_t, "runs", axis=0, tiled=True)
+    coeffs_full_t = jnp.concatenate(
+        lax.all_to_all(jnp.stack([coeffs_t] * lax.axis_size("runs")), "runs", 0, 0), axis=0
+    )
     peak_depth = lax.dot_general(
         sample_t, coeffs_full_t, (((0,), (1,)), ((), ())), preferred_element_type=jnp.float32
     ).astype(jnp.bfloat16)

time: 227 us -> 230 us (1.013)
  blocking collectives: 0 us -> 57.9 us
  waiting for transfers between devices: 193 us -> 140 us
  matrix products: 17.3 us -> 14.5 us
    all_to_all x0 -> x1, blocking collectives: none -> 57.9 us  [per_device(): lax.all_to_all(jnp.stack([coeffs_t] * lax.axis_size('runs')), 'runs', 0, 0)]
    all_gather x1 -> x0, waiting for transfers between devices: 52.7 us -> none  [per_device(): coeffs_full_t = lax.all_gather(coeffs_t, 'runs', axis=0, tiled=True)]
  transfers between devices with their start and end apart: 3 -> 2, of which waited for: 3 -> 2; matrix products, arithmetic and copies ran while one was open for 0% -> 0% of each run, Pallas kernels for 0% -> 0%
where the time goes in v1:
time: 230 us
  waiting for transfers between devices  140 us (61%)
  blocking collectives  57.9 us (25%)
  matrix products  14.5 us (6%)
  between operations  13.4 us (6%)
    reduce_scatter x1, waiting for transfers between devices, per_device(): lax.psum_scatter(partial_t, 'runs', scatter_dimension=0, tiled=True)  102 us
    all_to_all x1, blocking collectives, per_device(): lax.all_to_all(jnp.stack([coeffs_t] * lax.axis_size('runs')), 'runs', 0, 0)  57.9 us
    all_gather x1, waiting for transfers between devices, per_device(): both_full = lax.all_gather(both, 'cells', axis=0, tiled=False)  38.1 us
    dot_general x1, matrix products, per_device(): lax.dot_general(train_depth, train_t, (((0,), (1,)), ((), ())), preferred...  7.84 us
  transfers between devices with their start and end apart: 2, of which 2 were waited for; matrix products, arithmetic and copies ran while one was open for 0% of the time, Pallas kernels for 0%

profile of v1, /device:TPU:1, one launch (start us, length us, event | category | flops | bytes accessed | tf_op | source)
XLA Modules:
  0.0 229.5 jit_solution(2014881393588276899)
XLA Ops:
  6.5 0.0 copy-start
  6.5 0.0 all-gather.3.cloned.1.call-start
  6.5 1.6 maximum_bitcast_fusion
  8.2 0.0 all-gather.3.cloned.1.call-update
  8.2 0.0 reduce-scatter.2.cloned.1.call-start
  8.2 38.1 %all-gather.3.cloned.1.call-done = bf16[1024,512]{1,0:T(8,128)(2,1)} async-done(((bf16[128,512]{1,0:T(8,128)(2,1)}), bf16[1024,512]{1,0:T(8,128)(2,1)}) %all-gather.3.cloned.1.call-update) | async-done | bytes 1048592 | tf_op jit(solution)/shard_map/all_gather | solution.py:14
  46.3 1.3 fusion.3
  47.6 7.8 %convolution_bitcast_fusion = f32[4096,512]{0,1:T(8,128)} fusion(bf16[512,512]{1,0:T(8,128)(2,1)S(1)} %bitcast.14, bf16[512,4096]{1,0:T(8,128)(2,1)} %param.4), kind=kOutput, calls=%fused_computation | convolution fusion | flops 2147483648 | bytes 13107200 | tf_op jit(solution)/shard_map/dot_general | solution.py:17
  55.5 0.0 reduce-scatter.2.cloned.1.call-update
  55.5 102.2 %reduce-scatter.2.cloned.1.call-done = f32[128,512]{0,1:T(8,128)} async-done(((f32[4096,512]{0,1:T(8,128)}), f32[128,512]{0,1:T(8,128)}) %reduce-scatter.2.cloned.1.call-update) | async-done | bytes 262160 | tf_op jit(solution)/shard_map/reduce_scatter | solution.py:20
  157.7 0.0 copy-done
  157.7 2.2 convolution_convert_fusion.1
  159.9 0.5 stack.2
  160.3 57.9 %all_to_all.5 = bf16[32,128,512]{2,1,0:T(8,128)(2,1)S(1)} all-to-all(bf16[32,128,512]{2,1,0:T(8,128)(2,1)S(1)} %stack.2), channel_id=1, replica_groups=mesh['runs'=32,'cells'=8] {'runs'}, dimensions={0} | all-to-all | bytes 8388608 | tf_op jit(solution)/shard_map/all_to_all | solution.py:25
  218.3 4.4 %convolution_convert_fusion = bf16[512,4096]{1,0:T(8,128)(2,1)} fusion(bf16[512,512]{1,0:T(8,128)(2,1)S(1)} %bitcast.16, bf16[4096,512]{1,0:T(8,128)(2,1)S(1)} %bitcast.13), kind=kOutput, calls=%fused_computation.1 | convolution fusion | flops 2149580800 | bytes 8912896 | tf_op jit(solution)/shard_map/dot_general | solution.py:27
Async XLA Ops:
  6.5 151.1 %copy-start = (f32[512,512]{1,0:T(8,128)S(1)}, f32[512,512]{1,0:T(8,128)}, u32[]{:S(2)}) copy-start(f32[512,512]{1,0:T(8,128)} %param.7) | copy-start | bytes 3145732
  6.5 39.8 %all-gather.3.cloned.1.call-start = ((), (), s32[]{:S(2)}) async-start(), calls=%async_computation.3 | async-start | bytes 1179648 | tf_op jit(solution)/shard_map/all_gather | solution.py:14
  8.2 149.5 %reduce-scatter.2.cloned.1.call-start = ((), (), s32[]{:S(2)}) async-start(), calls=%async_computation.2 | async-start | bytes 8650752 | tf_op jit(solution)/shard_map/reduce_scatter | solution.py:20
Sparse Core Ops, SparseCore 0:
  9.1 37.1 all-gather.2
  55.6 102.0 reduce-scatter.1
